TPU v7x, 256 devices: a whole 4x4x8 slice. The times are simulated.
256 devices in a mesh: rows: 8 (over y, core), cols: 8 (over z), layers: 4 (over x).
Axes of the slice: x: 4, y: 4, z: 8, core: 2. Of those that a mesh axis runs over, the one named last changes fastest.
Arguments:
- y_blocks: bfloat16 [192, 32, 128, 128], P('rows', ('cols', 'layers')), may hold values from -1 to 1
- y_cols: int32 [192, 32], P('rows', ('cols', 'layers')), may hold values from 0 to 191, as said below
- prod_blocks: bfloat16 [192, 32, 128, 128], P('rows', ('cols', 'layers')), may hold values from -1 to 1
- prod_cols: int32 [192, 32], P('rows', ('cols', 'layers')), may hold values from 0 to 191, as said below
- out_cols: int32 [192, 32, 2], P('rows', ('cols', 'layers')), may hold values from 0 to 191, as said below
Outputs:
- y_next: bfloat16 [192, 32, 2, 128, 128], P('rows', ('cols', 'layers'))
Inputs may be any that keep to these rules, and one draw needn't show every extreme that they name: y_cols[i, t] lies in [t * 6, (t + 1) * 6): each block row of Y holds exactly one block in each range of 6 block columns. prod_cols[k, t] lies in [t * 6, (t + 1) * 6): each block row of M holds exactly one block in each range of 6 block columns. out_cols[i, t, :] are 2 distinct block columns in [t * 6, (t + 1) * 6), one of them equal to y_cols[i, t].
All inputs are finite; a program needn't handle non-finite values.
Results may differ from a plain program's by a relative error of at most 0.001.
Values may be sent and summed in bfloat16 or wider, within the bound.
No kernel may reach another device: no remote copies, remote signals or barrier semaphores. Data moves between devices by JAX's collectives and lax.ppermute only.
A program may use at most 128 MiB of HBM per device.

v0:
```python
import jax
import jax.numpy as jnp
from jax import lax
from jax.sharding import PartitionSpec as P

TILE_COLS = 6


def partial_products(
    running, shard_piece, lookup, lookup_cols, target_cols, layer_count, tile_cols
):
    left_all, left_cols = shard_piece
    block_rows, piece_len = left_cols.shape
    tile_count = target_cols.shape[1]
    outputs = block_rows * tile_count
    group_size = 1
    while group_size * 2 <= max(1, 64 // outputs) and piece_len % (group_size * 2) == 0:
        group_size = group_size * 2

    def advance(position, summed):
        offset = position * group_size
        left_blocks = lax.dynamic_slice_in_dim(left_all, offset, group_size, 1)
        inner_cols = lax.dynamic_slice_in_dim(left_cols, offset, group_size, 1)
        lookup_rows = inner_cols // (layer_count * tile_cols) * tile_cols + inner_cols % tile_cols
        right_blocks = lookup[lookup_rows]
        right_cols = lookup_cols[lookup_rows]
        present = (right_cols[:, :, :, None] == target_cols[:, None, :, :]).astype(jnp.float32)
        products = jnp.einsum(
            "igab,igtbc->igtac", left_blocks, right_blocks, preferred_element_type=jnp.float32
        )
        weighted = jnp.sum(products[:, :, :, None] * present[..., None, None], axis=1)
        return summed + weighted

    return lax.fori_loop(0, piece_len // group_size, advance, running)


def shards(y_blocks, y_cols, prod_blocks, prod_cols, out_cols):
    block_rows = y_blocks.shape[0]
    block_size = y_blocks.shape[2]
    out_width = out_cols.shape[2]
    tile_cols = TILE_COLS
    lookup, lookup_cols = (
        lax.all_gather(prod_blocks, "rows", axis=0, tiled=True),
        lax.all_gather(prod_cols, "rows", axis=0, tiled=True),
    )
    initial = jnp.zeros((block_rows, 1, out_width, block_size, block_size), jnp.float32)
    summed = partial_products(
        initial,
        (
            lax.all_gather(y_blocks, ("cols", "layers"), axis=1, tiled=True),
            lax.all_gather(y_cols, ("cols", "layers"), axis=1, tiled=True),
        ),
        lookup,
        lookup_cols,
        out_cols,
        1,
        tile_cols,
    )
    matches = out_cols == y_cols[:, :, None]
    own_blocks = jnp.where(matches[..., None, None], y_blocks[:, :, None].astype(jnp.float32), 0.0)
    updated = 1.5 * own_blocks - 0.5 * summed
    return updated.astype(jnp.bfloat16)


def solution(mesh):
    placed = (
        P("rows", ("cols", "layers"), None, None),
        P("rows", ("cols", "layers")),
        P("rows", ("cols", "layers"), None, None),
        P("rows", ("cols", "layers")),
        P("rows", ("cols", "layers"), None),
    )
    return jax.shard_map(
        shards,
        mesh=mesh,
        in_specs=placed,
        out_specs=P("rows", ("cols", "layers"), None, None, None),
        check_vma=False,
    )
```

profile of v0, /device:TPU:1, one launch (start us, length us, event | category | flops | bytes accessed | tf_op | source)
XLA Modules:
  0.0 567.5 jit_solution(7262077693090824826)
XLA Ops:
  10.6 36.9 %all-gather = s32[32,1,24]{2,1,0:T(1,128)S(1)} all-gather(s32[1,1,24]{2,1,0:T(1,128)} %bitcast.54), channel_id=1, replica_groups=mesh['rows'=8,'cols'=8,'layers'=4] {'cols','layers'}, dimensions={0}, use_global_device_ids=true | all-gather | bytes 3168 | tf_op jit(solution)/shard_map/all_gather | solution.py:51
  48.3 13.6 %all-reduce = s32[192]{0:T(256)S(1)} all-reduce(s32[192]{0:T(256)S(1)} %bitcast_dynamic-update-slice_fusion), channel_id=1, replica_groups=mesh['rows'=8,'cols'=8,'layers'=4] {'rows'}, use_global_device_ids=true, to_apply=%add | all-reduce | flops 192 | bytes 1536
  64.4 177.4 %all-gather.6.cloned.1.call-done = bf16[24,32,128,128]{3,2,1,0:T(8,128)(2,1)} async-done(((bf16[24,1,128,128]{3,2,1,0:T(8,128)(2,1)}), bf16[24,32,128,128]{3,2,1,0:T(8,128)(2,1)}) %all-gather.6.cloned.1.call-update) | async-done | bytes 25165840 | tf_op jit(solution)/shard_map/all_gather | solution.py:50
  241.8 314.7 %while.16 = (s32[]{:T(128)}, f32[24,1,2,128,128]{4,3,2,0,1:T(8,128)}, s32[24,32]{0,1:T(8,128)S(1)}, bf16[192,1,128,128]{3,2,1,0:T(8,128)(2,1)}, bf16[24,32,128,1...) while((s32[]{:T(128)}, ...), condition=%wide.region_2.3_spmd.clone, body=%wide.region_0.2_spmd.clone.sunk | while | flops 205260784 | bytes 31465964 | solution.py:34
  245.7 4.4 convolution_bitcast_fusion.2
  275.0 5.3 bitcast_add_fusion.2
  284.2 4.4 convolution_bitcast_fusion.2
  294.8 5.3 bitcast_add_fusion.2
  314.5 5.3 bitcast_add_fusion.2
  334.2 5.3 bitcast_add_fusion.2
  353.9 5.3 bitcast_add_fusion.2
  363.1 4.4 convolution_bitcast_fusion.2
  373.7 5.3 bitcast_add_fusion.2
  393.4 5.3 bitcast_add_fusion.2
  413.1 5.3 bitcast_add_fusion.2
  432.9 5.3 bitcast_add_fusion.2
  442.0 4.4 convolution_bitcast_fusion.2
  452.6 5.3 bitcast_add_fusion.2
  472.3 5.3 bitcast_add_fusion.2
  492.0 5.3 bitcast_add_fusion.2
  511.8 5.3 bitcast_add_fusion.2
  520.9 4.4 convolution_bitcast_fusion.2
  531.5 5.3 bitcast_add_fusion.2
  551.2 5.3 bitcast_add_fusion.2
  (219 shorter events, 223.3 us)
Async XLA Ops:
  6.5 235.3 %copy-start = (s32[24,1,2]{0,2,1:T(2,128)S(1)}, s32[24,1,2]{0,2,1:T(2,128)}, u32[]{:S(2)}) copy-start(s32[24,1,2]{0,2,1:T(2,128)} %param.11) | copy-start | bytes 580
  6.5 57.9 %all-gather.4.cloned.1.call-start = ((), (), s32[]{:S(2)}) async-start(), calls=%async_computation | async-start | bytes 7077888 | tf_op jit(solution)/shard_map/all_gather | solution.py:43
  7.3 234.6 %all-gather.6.cloned.1.call-start = ((), (), s32[]{:S(2)}) async-start(), calls=%async_computation.1 | async-start | bytes 25952256 | tf_op jit(solution)/shard_map/all_gather | solution.py:50
Sparse Core Ops, SparseCore 0:
  9.2 47.6 all-gather.3
  59.4 182.3 all-gather.5
where the time goes:
time: 569 us; the launch traced here: 567 us
  waiting for transfers between devices  179 us (31%)
  other arithmetic  136 us (24%)
  local copies, waits for them, and re-layouts  117 us (21%)
  matrix products  70.6 us (12%)
  blocking collectives  50.6 us (9%)
  between operations  14 us (2%)
    all_gather x1, waiting for transfers between devices, shards(): lax.all_gather(y_blocks, ('cols', 'layers'), axis=1, tiled=True)  177 us
    add x16, other arithmetic, advance(): return summed + weighted  83.7 us
    dot_general x16, matrix products, advance(): jnp.einsum('igab,igtbc->igtac', left_blocks, right_blocks, preferred_elem...  70.6 us
    gather x16, local copies, waits for them, and re-layouts, advance(): right_blocks = lookup[lookup_rows]  58.1 us
    reduce_sum x16, other arithmetic, advance(): jnp.sum(products[:, :, :, None] * present[..., None, None], axis=1)  43 us
    mul x16, local copies, waits for them, and re-layouts, advance(): products[:, :, :, None] * present[..., None, None]  38 us
    all_gather x1, blocking collectives, shards(): lax.all_gather(y_cols, ('cols', 'layers'), axis=1, tiled=True)  36.9 us
    unnamed x1, blocking collectives  13.6 us
  transfers between devices with their start and end apart: 2, of which 1 were waited for; matrix products, arithmetic and copies ran while one was open for 1% of the time, Pallas kernels for 0%

commit v1 on v0

--- a/solution.py
+++ b/solution.py
@@ -47,7 +47,15 @@
     summed = partial_products(
         initial,
         (
-            lax.all_gather(y_blocks, ("cols", "layers"), axis=1, tiled=True),
+            jnp.concatenate(
+                lax.all_to_all(
+                    jnp.stack([y_blocks for _ in range(lax.axis_size(("cols", "layers")))]),
+                    concat_axis=0,
+                    split_axis=0,
+                    axis_name=("cols", "layers"),
+                ),
+                axis=1,
+            ),
             lax.all_gather(y_cols, ("cols", "layers"), axis=1, tiled=True),
         ),
         lookup,

time: 569 us -> 996 us (1.75)
  blocking collectives: 50.6 us -> 635 us
  waiting for transfers between devices: 179 us -> 0.68 us
  starting transfers between devices: 0.04 us -> 12.2 us
    all_gather x1, blocking collectives: 36.9 us -> 620 us  [shards(): lax.all_gather(y_cols, ('cols', 'layers'), axis=1, tiled=True)]
    all_gather x1 -> x0, waiting for transfers between devices: 177 us -> none  [shards(): lax.all_gather(y_blocks, ('cols', 'layers'), axis=1, tiled=True)]
    all_to_all x0 -> x1, starting transfers between devices: none -> 12.1 us  [shards(): lax.all_to_all(jnp.stack([y_blocks for _ in range(lax.axis_size(('cols',...]
  transfers between devices with their start and end apart: 2 -> 2, of which waited for: 1 -> 0; matrix products, arithmetic and copies ran while one was open for 1% -> 0% of each run, Pallas kernels for 0% -> 0%
where the time goes in v1:
time: 996 us; the launch traced here: 993 us
  blocking collectives  635 us (64%)
  other arithmetic  134 us (13%)
  local copies, waits for them, and re-layouts  125 us (13%)
  matrix products  70.4 us (7%)
  between operations  14.2 us (1%)
  starting transfers between devices  12.2 us (1%)
    all_gather x1, blocking collectives, shards(): lax.all_gather(y_cols, ('cols', 'layers'), axis=1, tiled=True)  620 us
    add x16, other arithmetic, advance(): return summed + weighted  84 us
    dot_general x16, matrix products, advance(): jnp.einsum('igab,igtbc->igtac', left_blocks, right_blocks, preferred_elem...  70.4 us
    gather x16, local copies, waits for them, and re-layouts, advance(): right_blocks = lookup[lookup_rows]  58.1 us
    reduce_sum x16, other arithmetic, advance(): jnp.sum(products[:, :, :, None] * present[..., None, None], axis=1)  42.9 us
    mul x16, local copies, waits for them, and re-layouts, advance(): products[:, :, :, None] * present[..., None, None]  38 us
  transfers between devices with their start and end apart: 2, of which 0 were waited for; matrix products, arithmetic and copies ran while one was open for 0% of the time, Pallas kernels for 0%

profile of v1, /device:TPU:1, one launch (start us, length us, event | category | flops | bytes accessed | tf_op | source)
XLA Modules:
  0.0 993.1 jit_solution(1739323771541842713)
XLA Ops:
  6.5 9.9 stack.2
  16.4 12.1 %all-to-all-start = ((bf16[32,24,1,128,128]{4,3,1,2,0:T(8,128)(2,1)}), bf16[32,24,1,128,128]{4,3,1,2,0:T(8,128)(2,1)}, u32[]{:S(2)}, u32[]{:S(2)}) async-start(bf16[32,24,1,128,128]{4,3,1,2,0:T(8,128)(2,1)} %stack.2), calls=%async_computation | async-start | bytes 50331648 | tf_op jit(solution)/shard_map/all_to_all | solution.py:51
  30.8 620.1 %all-gather = s32[32,1,24]{2,1,0:T(1,128)S(1)} all-gather(s32[1,1,24]{2,1,0:T(1,128)S(1)} %bitcast.57), channel_id=1, replica_groups=mesh['rows'=8,'cols'=8,'layers'=4] {'cols','layers'}, dimensions={0}, use_global_device_ids=true | all-gather | bytes 3168 | tf_op jit(solution)/shard_map/all_gather | solution.py:59
  651.0 15.1 %all-reduce = s32[192]{0:T(256)S(1)} all-reduce(s32[192]{0:T(256)S(1)} %bitcast_dynamic-update-slice_fusion), channel_id=1, replica_groups=mesh['rows'=8,'cols'=8,'layers'=4] {'rows'}, use_global_device_ids=true, to_apply=%add | all-reduce | flops 192 | bytes 1536
  667.5 314.6 %while.16 = (s32[]{:T(128)}, f32[24,1,2,128,128]{4,3,2,0,1:T(8,128)}, s32[24,32]{0,1:T(8,128)S(1)}, bf16[192,1,128,128]{3,2,1,0:T(8,128)(2,1)}, bf16[24,32,128,1...) while((s32[]{:T(128)}, ...), condition=%wide.region_2.3_spmd.clone, body=%wide.region_0.2_spmd.clone.sunk | while | flops 205260784 | bytes 31465964 | solution.py:34
  671.4 4.4 convolution_bitcast_fusion.2
  690.1 4.4 convolution_bitcast_fusion.2
  700.7 5.3 bitcast_add_fusion.2
  720.4 5.3 bitcast_add_fusion.2
  740.1 5.3 bitcast_add_fusion.2
  749.3 4.4 convolution_bitcast_fusion.2
  759.8 5.3 bitcast_add_fusion.2
  779.6 5.3 bitcast_add_fusion.2
  799.3 5.3 bitcast_add_fusion.2
  819.0 5.3 bitcast_add_fusion.2
  828.2 4.4 convolution_bitcast_fusion.2
  838.7 5.3 bitcast_add_fusion.2
  858.5 5.3 bitcast_add_fusion.2
  878.2 5.3 bitcast_add_fusion.2
  897.9 5.3 bitcast_add_fusion.2
  917.6 5.3 bitcast_add_fusion.2
  937.3 5.3 bitcast_add_fusion.2
  957.1 5.3 bitcast_add_fusion.2
  976.8 5.3 bitcast_add_fusion.2
  (227 shorter events, 223.7 us)
Async XLA Ops:
  16.4 12.9 %copy-start.1 = (s32[24,1,2]{0,2,1:T(2,128)S(1)}, s32[24,1,2]{0,2,1:T(2,128)}, u32[]{:S(2)}) copy-start(s32[24,1,2]{0,2,1:T(2,128)} %param.11) | copy-start | bytes 580
  16.4 12.9 %copy-start.2 = (s32[24,1]{0,1:T(1,128)S(1)}, s32[24,1]{0,1:T(1,128)}, u32[]{:S(2)}) copy-start(s32[24,1]{0,1:T(1,128)} %param.8) | copy-start | bytes 292
  16.4 13.0 %copy-start.4 = (u32[256]{0:T(256)S(1)}, u32[256]{0:T(256)}, u32[]{:S(2)}) copy-start(u32[256]{0:T(256)} %constant.107) | copy-start | bytes 3076
  16.4 634.5 %copy-start.3 = (s32[24,1]{0,1:T(1,128)S(1)}, s32[24,1]{0,1:T(1,128)}, u32[]{:S(2)}) copy-start(s32[24,1]{0,1:T(1,128)} %param.10) | copy-start | bytes 292
  16.4 649.7 %copy-start = (bf16[24,1,128,128]{3,2,1,0:T(8,128)(2,1)S(1)}, bf16[24,1,128,128]{3,2,1,0:T(8,128)(2,1)}, u32[]{:S(2)}) copy-start(bf16[24,1,128,128]{3,2,1,0:T(8,128)(2,1)} %param.7) | copy-start | bytes 2359300
  16.4 651.0 %all-to-all-start = ((bf16[32,24,1,128,128]{4,3,1,2,0:T(8,128)(2,1)}), bf16[32,24,1,128,128]{4,3,1,2,0:T(8,128)(2,1)}, u32[]{:S(2)}, u32[]{:S(2)}) async-start(bf16[32,24,1,128,128]{4,3,1,2,0:T(8,128)(2,1)} %stack.2), calls=%async_computation | async-start | bytes 50331648 | tf_op jit(solution)/shard_map/all_to_all | solution.py:51
  28.6 638.9 %all-gather.3.cloned.1.call-start = ((), (), s32[]{:S(2)}) async-start(), calls=%async_computation.1 | async-start | bytes 7077888 | tf_op jit(solution)/shard_map/all_gather | solution.py:43
Sparse Core Ops, SparseCore 0:
  31.2 45.4 all-gather.2
